TPU v7x, 32 devices: a whole 2x2x4 slice. The times are simulated.
32 devices in a mesh: region: 2 (over y), tile: 4 (over z), corner: 2 (over x), kern: 2 (over core).
Axes of the slice: x: 2, y: 2, z: 4, core: 2. Of those that a mesh axis runs over, the one named last changes fastest.
Arguments:
- tile_mask: bfloat16 [16, 256, 256], P(('region', 'tile')), parts along dimension 0, may hold values from -1 to 1
- master_mask: bfloat16 [8, 256, 256], P(('region', 'tile')), parts along dimension 0, may hold values from -1 to 1
- target: bfloat16 [16, 256, 256], P(('region', 'tile')), parts along dimension 0, may hold values from 0 to 1
- inst_master: int32 [16], P(('region', 'tile')), parts along dimension 0, may hold values from 0 to 3, as said below
- inst_shift: int32 [16, 2], P(('region', 'tile')), parts along dimension 0, may hold values from 0 to 255
- kernels: float32 [2, 12, 2, 32, 32], P('corner'), may hold values from -24 to 24
- kernel_weight: float32 [2, 12], P('corner'), may hold values from 0.05 to 1
- corner_dose: float32 [2], P('corner'), may hold values from 0.6 to 1.6
Outputs:
- tile_grad: float32 [16, 256, 256], P(('region', 'tile')), parts along dimension 0
- master_grad: float32 [8, 256, 256], P(('region', 'tile')), parts along dimension 0
There are 2 independent parts, one for each index of `region`. A program takes and returns all parts, laid end to end along the dimension named above; an argument that names none is the same for every part. Nothing has to cross between parts.
Inputs may be any that keep to these rules, and one draw needn't show every extreme that they name: `inst_master`: each master cell is placed in exactly 2 tiles.
All inputs are finite; a program needn't handle non-finite values.
Results may differ from a plain program's by a relative error of at most 0.0003.
Values may be sent and summed in bfloat16 or wider, within the bound.
No kernel may reach another device: no remote copies, remote signals or barrier semaphores. Data moves between devices by JAX's collectives and lax.ppermute only.
A program may use at most 64 MiB of HBM per device.

v0:
```python
import math
import numpy as np
import jax
import jax.numpy as jnp
from jax import lax
from jax.sharding import PartitionSpec as P

P_SIZE = 256
B = 32
precise = lax.Precision.HIGHEST
steepness = 3.0
threshold = 1.0


def band_tables():
    freq = np.arange(B, dtype=np.int64) - B // 2
    pixel = np.arange(P_SIZE, dtype=np.int64)
    angle = (
        2.0 * math.pi / P_SIZE * np.mod(freq[:, None] * pixel[None, :], P_SIZE).astype(np.float64)
    )
    return (jnp.asarray(np.cos(angle), jnp.float32), jnp.asarray(-np.sin(angle), jnp.float32))


def phase_ramp(shift):
    freq = jnp.arange(B, dtype=jnp.int32) - B // 2
    total = (
        freq[None, :, None] * shift[:, 0][:, None, None]
        + freq[None, None, :] * shift[:, 1][:, None, None]
    )
    angle = 2.0 * math.pi / P_SIZE * jnp.mod(total, P_SIZE).astype(jnp.float32)
    return (jnp.cos(angle), -jnp.sin(angle))


def spectra(masks, cos_tab, sin_tab):
    rows_re = jnp.einsum("bx,nxy->nby", cos_tab, masks, precision=precise)
    rows_im = jnp.einsum("bx,nxy->nby", sin_tab, masks, precision=precise)
    spec_re = jnp.einsum("nby,cy->nbc", rows_re, cos_tab, precision=precise) - jnp.einsum(
        "nby,cy->nbc", rows_im, sin_tab, precision=precise
    )
    spec_im = jnp.einsum("nby,cy->nbc", rows_re, sin_tab, precision=precise) + jnp.einsum(
        "nby,cy->nbc", rows_im, cos_tab, precision=precise
    )
    return (spec_re, spec_im)


def back_pixels(x_re, x_im, cos_tab, sin_tab):
    half_re = jnp.einsum("bx,nbc->nxc", cos_tab, x_re, precision=precise) + jnp.einsum(
        "bx,nbc->nxc", sin_tab, x_im, precision=precise
    )
    half_im = jnp.einsum("bx,nbc->nxc", cos_tab, x_im, precision=precise) - jnp.einsum(
        "bx,nbc->nxc", sin_tab, x_re, precision=precise
    )
    return jnp.einsum("nxc,cy->nxy", half_re, cos_tab, precision=precise) + jnp.einsum(
        "nxc,cy->nxy", half_im, sin_tab, precision=precise
    )


def on_device(
    tile_mask, master_mask, target, inst_master, inst_shift, kernels, kernel_weight, corner_dose
):
    cos_tab, sin_tab = band_tables()
    scale = 1.0 / (P_SIZE * P_SIZE)
    local_tiles = tile_mask.shape[0]
    local_masters = master_mask.shape[0]
    tile_count = lax.axis_size("tile")
    tile_pos = lax.axis_index("tile")
    kern_count = lax.axis_size("kern")
    kern_pos = lax.axis_index("kern")
    per_dev = local_tiles // kern_count
    first = kern_pos * per_dev
    region_tiles = tile_count * local_tiles
    region_masters = tile_count * local_masters
    with jax.named_scope("master_spectra"):
        own_re, own_im = spectra(master_mask.astype(jnp.float32), cos_tab, sin_tab)
        own = jnp.stack([own_re, own_im], axis=1)
        every = lax.all_gather(own, "tile", axis=0, tiled=True)
    with jax.named_scope("tile_spectra"):
        mine_mask = lax.dynamic_slice_in_dim(tile_mask, first, per_dev, 0)
        goal = lax.dynamic_slice_in_dim(target, first, per_dev, 0).astype(jnp.float32)
        mine_master = lax.dynamic_slice_in_dim(inst_master, first, per_dev, 0)
        mine_shift = lax.dynamic_slice_in_dim(inst_shift, first, per_dev, 0)
        tile_re, tile_im = spectra(mine_mask.astype(jnp.float32), cos_tab, sin_tab)
        ph_re, ph_im = phase_ramp(mine_shift)
        pick = (
            mine_master[:, None] == jnp.arange(region_masters, dtype=jnp.int32)[None, :]
        ).astype(jnp.float32)
        sel = jnp.sum(pick[:, :, None, None, None] * every[None], axis=1)
        sel_re = sel[:, 0]
        sel_im = sel[:, 1]
        spec_re = tile_re + (ph_re * sel_re - ph_im * sel_im)
        spec_im = tile_im + (ph_re * sel_im + ph_im * sel_re)
    dose = corner_dose[0]
    h_re = kernels[0, :, 0]
    h_im = kernels[0, :, 1]
    weights = kernel_weight[0]
    with jax.named_scope("forward_fields"):
        x_re = h_re[:, None] * spec_re[None] - h_im[:, None] * spec_im[None]
        x_im = h_re[:, None] * spec_im[None] + h_im[:, None] * spec_re[None]
        half_re = jnp.einsum("bx,knbc->knxc", cos_tab, x_re, precision=precise) + jnp.einsum(
            "bx,knbc->knxc", sin_tab, x_im, precision=precise
        )
        half_im = jnp.einsum("bx,knbc->knxc", cos_tab, x_im, precision=precise) - jnp.einsum(
            "bx,knbc->knxc", sin_tab, x_re, precision=precise
        )
        f_re = (
            jnp.einsum("knxc,cy->knxy", half_re, cos_tab, precision=precise)
            + jnp.einsum("knxc,cy->knxy", half_im, sin_tab, precision=precise)
        ) * scale
        f_im = (
            jnp.einsum("knxc,cy->knxy", half_im, cos_tab, precision=precise)
            - jnp.einsum("knxc,cy->knxy", half_re, sin_tab, precision=precise)
        ) * scale
    with jax.named_scope("resist_sensitivity"):
        intensity = jnp.sum(weights[:, None, None, None] * (f_re * f_re + f_im * f_im), axis=0)
        resist = jax.nn.sigmoid(steepness * (dose * intensity - threshold))
        sens = 2.0 * (resist - goal) * resist * (1.0 - resist) * steepness * dose
    with jax.named_scope("adjoint_spectra"):
        g_re = (2.0 * weights)[:, None, None, None] * sens[None] * f_re
        g_im = (2.0 * weights)[:, None, None, None] * sens[None] * f_im
        mid_re = jnp.einsum("knxy,cy->knxc", g_re, cos_tab, precision=precise) - jnp.einsum(
            "knxy,cy->knxc", g_im, sin_tab, precision=precise
        )
        mid_im = jnp.einsum("knxy,cy->knxc", g_re, sin_tab, precision=precise) + jnp.einsum(
            "knxy,cy->knxc", g_im, cos_tab, precision=precise
        )
        out_re = (
            jnp.einsum("bx,knxc->knbc", cos_tab, mid_re, precision=precise)
            - jnp.einsum("bx,knxc->knbc", sin_tab, mid_im, precision=precise)
        ) * scale
        out_im = (
            jnp.einsum("bx,knxc->knbc", cos_tab, mid_im, precision=precise)
            + jnp.einsum("bx,knxc->knbc", sin_tab, mid_re, precision=precise)
        ) * scale
        grad_re = jnp.sum(h_re[:, None] * out_re + h_im[:, None] * out_im, axis=0)
        grad_im = jnp.sum(h_re[:, None] * out_im - h_im[:, None] * out_re, axis=0)
    with jax.named_scope("gradient_exchange"):
        back_re = ph_re * grad_re + ph_im * grad_im
        back_im = ph_re * grad_im - ph_im * grad_re
        tile_slot = tile_pos * local_tiles + first + jnp.arange(per_dev, dtype=jnp.int32)
        tile_pick = (
            tile_slot[:, None] == jnp.arange(region_tiles, dtype=jnp.int32)[None, :]
        ).astype(jnp.float32)
        own_grad = jnp.stack([grad_re, grad_im], axis=1)
        own_back = jnp.stack([back_re, back_im], axis=1)
        tile_part = jnp.sum(tile_pick[:, :, None, None, None] * own_grad[:, None], axis=0)
        master_part = jnp.sum(pick[:, :, None, None, None] * own_back[:, None], axis=0)
        slots = jnp.concatenate([tile_part, master_part], axis=0)
        summed = lax.psum(slots, ("tile", "corner", "kern"))
        mine_tiles = lax.dynamic_slice_in_dim(summed, tile_pos * local_tiles, local_tiles, 0)
        mine_masters = lax.dynamic_slice_in_dim(
            summed, region_tiles + tile_pos * local_masters, local_masters, 0
        )
    with jax.named_scope("pixel_gradients"):
        tile_grad = back_pixels(mine_tiles[:, 0], mine_tiles[:, 1], cos_tab, sin_tab)
        master_grad = back_pixels(mine_masters[:, 0], mine_masters[:, 1], cos_tab, sin_tab)
    return (tile_grad, master_grad)


def solution(mesh):
    return jax.shard_map(
        on_device,
        mesh=mesh,
        in_specs=(
            P(("region", "tile"), None, None),
            P(("region", "tile"), None, None),
            P(("region", "tile"), None, None),
            P(("region", "tile")),
            P(("region", "tile"), None),
            P("corner", None, None, None, None),
            P("corner", None),
            P("corner"),
        ),
        out_specs=(P(("region", "tile"), None, None), P(("region", "tile"), None, None)),
        check_vma=False,
    )
```

profile of v0, /device:TPU:0, one launch (start us, length us, event | category | flops | bytes accessed | tf_op | source)
XLA Modules:
  0.0 185.2 jit_solution(1260496238623281663)
XLA Ops:
  7.3 1.1 fusion.41
  8.4 1.1 fusion.39
  11.4 1.0 convolution_bitcast_fusion.1
  12.4 1.0 convolution_bitcast_fusion
  16.5 1.3 dynamic_slice.20
  20.4 15.1 %all_gather.3 = f32[4,2,32,32]{3,2,1,0:T(8,128)S(1)} all-gather(f32[1,2,32,32]{3,2,1,0:T(8,128)S(1)} %pad_maximum_fusion.1), channel_id=1, replica_groups=mesh['region'=2,'tile'=4,'corner'=2,'kern'=2] {'tile'}, dimensions={0}, use_global_device_ids=true | all-gather | bytes 40960 | tf_op jit(solution)/shard_map/master_spectra/all_gather | solution.py:76
  35.4 1.3 fusion.75
  38.8 1.1 fusion.77
  42.0 2.7 %fusion.83 = f32[12,256,256]{2,1,0:T(8,128)S(1)} fusion(f32[12,256,32]{1,2,0:T(8,128)S(1)} %fusion.15, f32[32,256,1]{1,0,2:T(8,128)S(1)} %copy-done.6), kind=kOutput, calls=%fused_computation.143 | convolution fusion | flops 301989888 | bytes 3571712 | tf_op jit(solution)/shard_map/forward_fields/knxc,cy->knxy/dot_general | solution.py:106
  44.8 4.3 %fusion.84 = f32[12,256,256]{2,1,0:T(8,128)} fusion(f32[12,256,32]{1,2,0:T(8,128)S(1)} %fusion.14, f32[32,256,1]{1,0,2:T(8,128)S(1)} %copy-done.6), kind=kOutput, calls=%fused_computation.144 | convolution fusion | flops 301989888 | bytes 3571712 | tf_op jit(solution)/shard_map/forward_fields/knxc,cy->knxy/dot_general | solution.py:110
  49.1 2.7 %add_multiply_fusion = f32[12,256,256]{2,1,0:T(8,128)S(1)} fusion(f32[12,256,256]{2,1,0:T(8,128)S(1)} %fusion.83, f32[12,256,32]{1,2,0:T(8,128)S(1)} %fusion.14, f32[32,256,1]{1,0,2:T(8,128)S(1)} %copy-done.5), kind=kOutput, calls=%fused_computation.4 | convolution fusion | flops 303562752 | bytes 6717440 | tf_op jit(solution)/shard_map/forward_fields/knxc,cy->knxy/dot_general | solution.py:107
  52.5 5.6 %multiply_reduce_fusion = (f32[256,256]{1,0:T(8,128)S(1)}, f32[12,256,256]{2,1,0:T(8,128)S(1)}) fusion(f32[12,256,256]{2,1,0:T(8,128)S(1)} %add_multiply_fusion, f32[12]{0:T(128)S(1)} %bitcast.235, f32[12,256,256]{2,1,0:T(8,128)} %fusion.84, f32[12,256,32]{1,2,0:T(8,128)} %copy-done.7, f32[32,256,1]{1,0,2:T(8,128)S(1)} %copy-done.5), kind=kOutput, calls=%fused_computation.2 | convolution fusion | flops 307429376 | bytes 10125360 | tf_op jit(solution)/shard_map/forward_fields/knxc,cy->knxy/dot_general | solution.py:111
  58.3 3.3 %fusion = f32[12,256,32]{1,2,0:T(8,128)S(1)} fusion(f32[32,256,1]{1,0,2:T(8,128)S(1)} %copy-done.5, f32[12,256,256]{2,1,0:T(8,128)S(1)} %add_multiply_fusion, f32[256,256]{1,0:T(8,128)S(1)} %fusion.32, f32[12]{0:T(128)S(1)} %broadcast_multiply_fusion.2), kind=kOutput, calls=%fused_computation.5 | convolution fusion | flops 303562752 | bytes 3833904 | tf_op jit(solution)/shard_map/adjoint_spectra/knxy,cy->knxc/dot_general | solution.py:123
  61.6 3.3 %fusion.1 = f32[12,256,32]{1,2,0:T(8,128)S(1)} fusion(f32[32,256,1]{1,0,2:T(8,128)S(1)} %copy-done.6, f32[12,256,256]{2,1,0:T(8,128)S(1)} %add_multiply_fusion, f32[256,256]{1,0:T(8,128)S(1)} %fusion.32, f32[12]{0:T(128)S(1)} %broadcast_multiply_fusion.2), kind=kOutput, calls=%fused_computation.6 | convolution fusion | flops 303562752 | bytes 3833904 | tf_op jit(solution)/shard_map/adjoint_spectra/knxy,cy->knxc/dot_general | solution.py:120
  64.8 3.3 %fusion.13 = f32[12,256,32]{1,2,0:T(8,128)S(1)} fusion(f32[12,256,32]{1,2,0:T(8,128)S(1)} %fusion, f32[32,256,1]{1,0,2:T(8,128)S(1)} %copy-done.6, f32[12,256,256]{2,1,0:T(8,128)S(1)} %get-tuple-element.11, f32[256,256]{1,0:T(8,128)S(1)} %fusion.32, f32[12]{0:T(128)S(1)} %broadcast_multiply_fusion.2), kind=kOutput, calls=%fused_computation.19 | convolution fusion | flops 303661056 | bytes 4227120 | tf_op jit(solution)/shard_map/adjoint_spectra/knxy,cy->knxc/dot_general | solution.py:123
  68.2 3.5 %fusion.12 = f32[12,256,32]{1,2,0:T(8,128)S(1)} fusion(f32[12,256,32]{1,2,0:T(8,128)S(1)} %fusion.1, f32[32,256,1]{1,0,2:T(8,128)S(1)} %copy-done.5, f32[12,256,256]{2,1,0:T(8,128)S(1)} %get-tuple-element.11, f32[256,256]{1,0:T(8,128)S(1)} %fusion.32, f32[12]{0:T(128)S(1)} %broadcast_multiply_fusion.2), kind=kOutput, calls=%fused_computation.18 | convolution fusion | flops 303661056 | bytes 4227120 | tf_op jit(solution)/shard_map/adjoint_spectra/knxy,cy->knxc/dot_general | solution.py:120
  74.9 91.9 %all-reduce.2.cloned.1.call-done = f32[12,2,32,32]{3,2,1,0:T(8,128)} async-done(((f32[12,2,32,32]{3,2,1,0:T(8,128)}), f32[12,2,32,32]{3,2,1,0:T(8,128)}) %all-reduce.2.cloned.1.call-update) | async-done | bytes 98320 | tf_op jit(solution)/shard_map/gradient_exchange/psum | solution.py:148
  167.8 0.9 fusion.24
  169.2 1.0 fusion.53
  170.2 1.0 fusion.22
  173.7 1.1 fusion.16
  174.9 1.0 fusion.54
  175.9 1.0 fusion.21
  176.9 1.4 convolution_add_fusion
  (67 shorter events, 18.8 us)
Async XLA Ops:
  7.2 4.2 %copy-start = (bf16[2,256,256]{2,1,0:T(8,128)(2,1)S(1)}, bf16[2,256,256]{2,1,0:T(8,128)(2,1)}, u32[]{:S(2)}) copy-start(bf16[2,256,256]{2,1,0:T(8,128)(2,1)} %param.10) | copy-start | bytes 786436
  7.2 33.0 %copy-start.6 = (f32[32,256,1]{1,0,2:T(8,128)S(1)}, f32[32,256,1]{1,0,2:T(8,128)}, u32[]{:S(2)}) copy-start(f32[32,256,1]{1,0,2:T(8,128)} %constant.68) | copy-start | bytes 98308
  7.2 33.9 %copy-start.5 = (f32[32,256,1]{1,0,2:T(8,128)S(1)}, f32[32,256,1]{1,0,2:T(8,128)}, u32[]{:S(2)}) copy-start(f32[32,256,1]{1,0,2:T(8,128)} %constant.69) | copy-start | bytes 98308
  7.2 159.6 %all-reduce.2.cloned.1.call-start = ((), (), s32[]{:S(2)}) async-start(), calls=%async_computation | async-start | bytes 786432 | tf_op jit(solution)/shard_map/gradient_exchange/psum | solution.py:148
  40.0 4.8 %copy-start.1 = (f32[1,12,1,32,32]{3,4,1,2,0:T(8,128)}, f32[1,12,1,32,32]{3,4,1,2,0:T(8,128)S(1)}, u32[]{:S(2)}) copy-start(f32[1,12,1,32,32]{3,4,1,2,0:T(8,128)S(1)} %copy.22) | copy-start | bytes 147460
  40.1 4.6 %copy-start.3 = (f32[1,12,1,32,32]{3,4,1,2,0:T(8,128)}, f32[1,12,1,32,32]{3,4,1,2,0:T(8,128)S(1)}, u32[]{:S(2)}) copy-start(f32[1,12,1,32,32]{3,4,1,2,0:T(8,128)S(1)} %copy.23) | copy-start | bytes 147460
  42.0 2.8 %copy-start.7 = (f32[12,256,32]{1,2,0:T(8,128)}, f32[12,256,32]{1,2,0:T(8,128)S(1)}, u32[]{:S(2)}) copy-start(f32[12,256,32]{1,2,0:T(8,128)S(1)} %fusion.15) | copy-start | bytes 1179652
  49.1 3.4 %copy-start.11 = (f32[1,12]{1,0:T(1,128)S(1)}, f32[1,12]{1,0:T(1,128)}, u32[]{:S(2)}) copy-start(f32[1,12]{1,0:T(1,128)} %param.16) | copy-start | bytes 148
  52.5 5.6 %copy-start.10 = (bf16[2,256,256]{2,1,0:T(8,128)(2,1)S(1)}, bf16[2,256,256]{2,1,0:T(8,128)(2,1)}, u32[]{:S(2)}) copy-start(bf16[2,256,256]{2,1,0:T(8,128)(2,1)} %param.12) | copy-start | bytes 786436
  68.1 4.9 %copy-start.2 = (f32[1,12,1,32,32]{3,4,1,2,0:T(8,128)S(1)}, f32[1,12,1,32,32]{3,4,1,2,0:T(8,128)}, u32[]{:S(2)}) copy-start(f32[1,12,1,32,32]{3,4,1,2,0:T(8,128)} %copy-done.1) | copy-start | bytes 147460
  68.1 4.9 %copy-start.4 = (f32[1,12,1,32,32]{3,4,1,2,0:T(8,128)S(1)}, f32[1,12,1,32,32]{3,4,1,2,0:T(8,128)}, u32[]{:S(2)}) copy-start(f32[1,12,1,32,32]{3,4,1,2,0:T(8,128)} %copy-done.3) | copy-start | bytes 147460
  71.6 95.2 %copy-start.9 = (f32[32,256]{1,0:T(8,128)S(1)}, f32[32,256]{1,0:T(8,128)}, u32[]{:S(2)}) copy-start(f32[32,256]{1,0:T(8,128)} %constant.58.clone) | copy-start | bytes 98308
  71.7 96.1 %copy-start.8 = (f32[32,256]{1,0:T(8,128)S(1)}, f32[32,256]{1,0:T(8,128)}, u32[]{:S(2)}) copy-start(f32[32,256]{1,0:T(8,128)} %constant.59.clone) | copy-start | bytes 98308
Sparse Core Ops, SparseCore 0:
  75.0 91.7 all-reduce.1
where the time goes:
time: 187 us; the launch traced here: 185 us
  waiting for transfers between devices  91.9 us (49%)
  matrix products  55.3 us (30%)
  between operations  15.2 us (8%)
  blocking collectives  15.1 us (8%)
  local copies, waits for them, and re-layouts  4.24 us (2%)
  other arithmetic  3.34 us (2%)
    psum x1, waiting for transfers between devices, on_device(): summed = lax.psum(slots, ('tile', 'corner', 'kern'))  91.9 us
    all_gather x1, blocking collectives, on_device(): every = lax.all_gather(own, 'tile', axis=0, tiled=True)  15.1 us
    dot_general x1, matrix products, on_device(): jnp.einsum('knxc,cy->knxy', half_re, sin_tab, precision=precise)  5.58 us
    dot_general x1, matrix products, on_device(): jnp.einsum('knxc,cy->knxy', half_im, cos_tab, precision=precise)  4.34 us
  transfers between devices with their start and end apart: 1, of which 1 were waited for; matrix products, arithmetic and copies ran while one was open for 0% of the time, Pallas kernels for 0%

commit v1 on v0

--- a/solution.py
+++ b/solution.py
@@ -145,7 +145,11 @@
         tile_part = jnp.sum(tile_pick[:, :, None, None, None] * own_grad[:, None], axis=0)
         master_part = jnp.sum(pick[:, :, None, None, None] * own_back[:, None], axis=0)
         slots = jnp.concatenate([tile_part, master_part], axis=0)
-        summed = lax.psum(slots, ("tile", "corner", "kern"))
+
+        def _handle_task(inp, dev_axis):
+            return jax.lax.all_gather(inp, axis_name=dev_axis).sum(axis=0)
+
+        summed = _handle_task(slots, ("tile", "corner", "kern"))
         mine_tiles = lax.dynamic_slice_in_dim(summed, tile_pos * local_tiles, local_tiles, 0)
         mine_masters = lax.dynamic_slice_in_dim(
             summed, region_tiles + tile_pos * local_masters, local_masters, 0

time: 187 us -> 155 us (0.83)
  waiting for transfers between devices: 91.9 us -> 63.4 us
  matrix products: 55.3 us -> 49.4 us
  other arithmetic: 3.34 us -> 6.94 us
    psum x1 -> x0, waiting for transfers between devices: 91.9 us -> none  [on_device(): summed = lax.psum(slots, ('tile', 'corner', 'kern'))]
    all_gather x0 -> x1, waiting for transfers between devices: none -> 63.3 us  [_handle_task(): return jax.lax.all_gather(inp, axis_name=dev_axis).sum(axis=0)]
    reduce_sum x0 -> x1, other arithmetic: none -> 3.6 us  [_handle_task(): return jax.lax.all_gather(inp, axis_name=dev_axis).sum(axis=0)]
where the time goes in v1:
time: 155 us; the launch traced here: 154 us
  waiting for transfers between devices  63.4 us (41%)
  matrix products  49.4 us (32%)
  between operations  15.2 us (10%)
  blocking collectives  15.1 us (10%)
  other arithmetic  6.94 us (4%)
  local copies, waits for them, and re-layouts  4.23 us (3%)
    all_gather x1, waiting for transfers between devices, _handle_task(): return jax.lax.all_gather(inp, axis_name=dev_axis).sum(axis=0)  63.3 us
    all_gather x1, blocking collectives, on_device(): every = lax.all_gather(own, 'tile', axis=0, tiled=True)  15.1 us
    dot_general x1, matrix products, on_device(): jnp.einsum('knxc,cy->knxy', half_re, sin_tab, precision=precise)  5.59 us
    dot_general x1, matrix products, on_device(): jnp.einsum('knxc,cy->knxy', half_im, cos_tab, precision=precise)  4.34 us
    reduce_sum x1, other arithmetic, _handle_task(): return jax.lax.all_gather(inp, axis_name=dev_axis).sum(axis=0)  3.6 us
    dot_general x1, matrix products, on_device(): jnp.einsum('knxy,cy->knxc', g_im, sin_tab, precision=precise)  3.49 us
    dot_general x1, matrix products, on_device(): jnp.einsum('knxy,cy->knxc', g_im, cos_tab, precision=precise)  3.27 us
    dot_general x1, matrix products, on_device(): jnp.einsum('knxy,cy->knxc', g_re, cos_tab, precision=precise)  3.27 us
  transfers between devices with their start and end apart: 1, of which 1 were waited for; matrix products, arithmetic and copies ran while one was open for 0% of the time, Pallas kernels for 0%

profile of v1, /device:TPU:0, one launch (start us, length us, event | category | flops | bytes accessed | tf_op | source)
XLA Modules:
  0.0 154.3 jit_solution(9931831129123140346)
XLA Ops:
  7.3 1.1 fusion.41
  8.4 1.1 fusion.39
  11.4 1.0 convolution_bitcast_fusion.1
  12.4 1.0 convolution_bitcast_fusion
  16.5 1.3 dynamic_slice.20
  18.5 0.9 fusion.26
  19.4 0.9 fusion.27
  20.4 15.1 %all_gather.9 = f32[4,2,32,32]{3,2,1,0:T(8,128)S(1)} all-gather(f32[1,2,32,32]{3,2,1,0:T(8,128)S(1)} %pad_maximum_fusion.1), channel_id=1, replica_groups=mesh['region'=2,'tile'=4,'corner'=2,'kern'=2] {'tile'}, dimensions={0}, use_global_device_ids=true | all-gather | bytes 40960 | tf_op jit(solution)/shard_map/master_spectra/all_gather | solution.py:76
  35.4 1.3 fusion.75
  36.8 0.9 fusion.28
  37.8 0.9 fusion.25
  38.8 1.1 fusion.77
  42.0 2.7 %fusion.83 = f32[12,256,256]{2,1,0:T(8,128)S(1)} fusion(f32[12,256,32]{1,2,0:T(8,128)S(1)} %fusion.15, f32[32,256,1]{1,0,2:T(8,128)S(1)} %copy-done.6), kind=kOutput, calls=%fused_computation.143 | convolution fusion | flops 301989888 | bytes 3571712 | tf_op jit(solution)/shard_map/forward_fields/knxc,cy->knxy/dot_general | solution.py:106
  44.8 4.3 %fusion.84 = f32[12,256,256]{2,1,0:T(8,128)} fusion(f32[12,256,32]{1,2,0:T(8,128)S(1)} %fusion.14, f32[32,256,1]{1,0,2:T(8,128)S(1)} %copy-done.6), kind=kOutput, calls=%fused_computation.144 | convolution fusion | flops 301989888 | bytes 3571712 | tf_op jit(solution)/shard_map/forward_fields/knxc,cy->knxy/dot_general | solution.py:110
  49.1 2.7 %add_multiply_fusion = f32[12,256,256]{2,1,0:T(8,128)S(1)} fusion(f32[12,256,256]{2,1,0:T(8,128)S(1)} %fusion.83, f32[12,256,32]{1,2,0:T(8,128)S(1)} %fusion.14, f32[32,256,1]{1,0,2:T(8,128)S(1)} %copy-done.5), kind=kOutput, calls=%fused_computation.4 | convolution fusion | flops 303562752 | bytes 6717440 | tf_op jit(solution)/shard_map/forward_fields/knxc,cy->knxy/dot_general | solution.py:107
  52.5 5.6 %multiply_reduce_fusion = (f32[256,256]{1,0:T(8,128)S(1)}, f32[12,256,256]{2,1,0:T(8,128)S(1)}) fusion(f32[12,256,256]{2,1,0:T(8,128)S(1)} %add_multiply_fusion, f32[12]{0:T(128)S(1)} %bitcast.237, f32[12,256,256]{2,1,0:T(8,128)} %fusion.84, f32[12,256,32]{1,2,0:T(8,128)} %copy-done.7, f32[32,256,1]{1,0,2:T(8,128)S(1)} %copy-done.5), kind=kOutput, calls=%fused_computation.2 | convolution fusion | flops 307429376 | bytes 10125360 | tf_op jit(solution)/shard_map/forward_fields/knxc,cy->knxy/dot_general | solution.py:111
  58.3 3.3 %fusion = f32[12,256,32]{1,2,0:T(8,128)S(1)} fusion(f32[32,256,1]{1,0,2:T(8,128)S(1)} %copy-done.5, f32[12,256,256]{2,1,0:T(8,128)S(1)} %add_multiply_fusion, f32[256,256]{1,0:T(8,128)S(1)} %fusion.32, f32[12]{0:T(128)S(1)} %broadcast_multiply_fusion.2), kind=kOutput, calls=%fused_computation.5 | convolution fusion | flops 303562752 | bytes 3833904 | tf_op jit(solution)/shard_map/adjoint_spectra/knxy,cy->knxc/dot_general | solution.py:123
  61.6 3.3 %fusion.1 = f32[12,256,32]{1,2,0:T(8,128)S(1)} fusion(f32[32,256,1]{1,0,2:T(8,128)S(1)} %copy-done.6, f32[12,256,256]{2,1,0:T(8,128)S(1)} %add_multiply_fusion, f32[256,256]{1,0:T(8,128)S(1)} %fusion.32, f32[12]{0:T(128)S(1)} %broadcast_multiply_fusion.2), kind=kOutput, calls=%fused_computation.6 | convolution fusion | flops 303562752 | bytes 3833904 | tf_op jit(solution)/shard_map/adjoint_spectra/knxy,cy->knxc/dot_general | solution.py:120
  64.8 3.3 %fusion.13 = f32[12,256,32]{1,2,0:T(8,128)S(1)} fusion(f32[12,256,32]{1,2,0:T(8,128)S(1)} %fusion, f32[32,256,1]{1,0,2:T(8,128)S(1)} %copy-done.6, f32[12,256,256]{2,1,0:T(8,128)S(1)} %get-tuple-element.11, f32[256,256]{1,0:T(8,128)S(1)} %fusion.32, f32[12]{0:T(128)S(1)} %broadcast_multiply_fusion.2), kind=kOutput, calls=%fused_computation.19 | convolution fusion | flops 303661056 | bytes 4227120 | tf_op jit(solution)/shard_map/adjoint_spectra/knxy,cy->knxc/dot_general | solution.py:123
  68.2 3.5 %fusion.12 = f32[12,256,32]{1,2,0:T(8,128)S(1)} fusion(f32[12,256,32]{1,2,0:T(8,128)S(1)} %fusion.1, f32[32,256,1]{1,0,2:T(8,128)S(1)} %copy-done.5, f32[12,256,256]{2,1,0:T(8,128)S(1)} %get-tuple-element.11, f32[256,256]{1,0:T(8,128)S(1)} %fusion.32, f32[12]{0:T(128)S(1)} %broadcast_multiply_fusion.2), kind=kOutput, calls=%fused_computation.18 | convolution fusion | flops 303661056 | bytes 4227120 | tf_op jit(solution)/shard_map/adjoint_spectra/knxy,cy->knxc/dot_general | solution.py:120
  74.9 63.3 %all-gather.3.cloned.1.call-done = f32[192,2,32,32]{3,2,1,0:T(8,128)} async-done(((f32[12,2,32,32]{3,2,1,0:T(8,128)}), f32[192,2,32,32]{3,2,1,0:T(8,128)}) %all-gather.3.cloned.1.call-update) | async-done | bytes 1572880 | tf_op jit(solution)/shard_map/gradient_exchange/all_gather | solution.py:150
  138.2 3.6 %reduce_sum.60 = f32[12,2,32,32]{3,2,1,0:T(8,128)S(1)} reduce(f32[16,12,2,32,32]{4,3,2,1,0:T(8,128)} %bitcast.232, f32[]{:T(128)} %constant.51.clone.1), dimensions={0}, to_apply=%region_4.5 | reduce | flops 368640 | bytes 1671172 | tf_op jit(solution)/shard_map/gradient_exchange/reduce_sum | solution.py:150
  144.9 1.1 fusion.16
  146.0 1.4 convolution_add_fusion
  (68 shorter events, 14.3 us)
Async XLA Ops:
  7.2 4.2 %copy-start = (bf16[2,256,256]{2,1,0:T(8,128)(2,1)S(1)}, bf16[2,256,256]{2,1,0:T(8,128)(2,1)}, u32[]{:S(2)}) copy-start(bf16[2,256,256]{2,1,0:T(8,128)(2,1)} %param.10) | copy-start | bytes 786436
  7.2 33.0 %copy-start.6 = (f32[32,256,1]{1,0,2:T(8,128)S(1)}, f32[32,256,1]{1,0,2:T(8,128)}, u32[]{:S(2)}) copy-start(f32[32,256,1]{1,0,2:T(8,128)} %constant.68) | copy-start | bytes 98308
  7.2 33.9 %copy-start.5 = (f32[32,256,1]{1,0,2:T(8,128)S(1)}, f32[32,256,1]{1,0,2:T(8,128)}, u32[]{:S(2)}) copy-start(f32[32,256,1]{1,0,2:T(8,128)} %constant.69) | copy-start | bytes 98308
  7.2 131.0 %all-gather.3.cloned.1.call-start = ((), (), s32[]{:S(2)}) async-start(), calls=%async_computation | async-start | bytes 6684672 | tf_op jit(solution)/shard_map/gradient_exchange/all_gather | solution.py:150
  40.0 4.8 %copy-start.1 = (f32[1,12,1,32,32]{3,4,1,2,0:T(8,128)}, f32[1,12,1,32,32]{3,4,1,2,0:T(8,128)S(1)}, u32[]{:S(2)}) copy-start(f32[1,12,1,32,32]{3,4,1,2,0:T(8,128)S(1)} %copy.22) | copy-start | bytes 147460
  40.1 4.6 %copy-start.3 = (f32[1,12,1,32,32]{3,4,1,2,0:T(8,128)}, f32[1,12,1,32,32]{3,4,1,2,0:T(8,128)S(1)}, u32[]{:S(2)}) copy-start(f32[1,12,1,32,32]{3,4,1,2,0:T(8,128)S(1)} %copy.23) | copy-start | bytes 147460
  42.0 2.8 %copy-start.7 = (f32[12,256,32]{1,2,0:T(8,128)}, f32[12,256,32]{1,2,0:T(8,128)S(1)}, u32[]{:S(2)}) copy-start(f32[12,256,32]{1,2,0:T(8,128)S(1)} %fusion.15) | copy-start | bytes 1179652
  49.1 3.4 %copy-start.11 = (f32[1,12]{1,0:T(1,128)S(1)}, f32[1,12]{1,0:T(1,128)}, u32[]{:S(2)}) copy-start(f32[1,12]{1,0:T(1,128)} %param.16) | copy-start | bytes 148
  52.5 5.6 %copy-start.10 = (bf16[2,256,256]{2,1,0:T(8,128)(2,1)S(1)}, bf16[2,256,256]{2,1,0:T(8,128)(2,1)}, u32[]{:S(2)}) copy-start(bf16[2,256,256]{2,1,0:T(8,128)(2,1)} %param.12) | copy-start | bytes 786436
  68.1 4.9 %copy-start.2 = (f32[1,12,1,32,32]{3,4,1,2,0:T(8,128)S(1)}, f32[1,12,1,32,32]{3,4,1,2,0:T(8,128)}, u32[]{:S(2)}) copy-start(f32[1,12,1,32,32]{3,4,1,2,0:T(8,128)} %copy-done.1) | copy-start | bytes 147460
  68.1 4.9 %copy-start.4 = (f32[1,12,1,32,32]{3,4,1,2,0:T(8,128)S(1)}, f32[1,12,1,32,32]{3,4,1,2,0:T(8,128)}, u32[]{:S(2)}) copy-start(f32[1,12,1,32,32]{3,4,1,2,0:T(8,128)} %copy-done.3) | copy-start | bytes 147460
  138.2 3.6 %copy-start.9 = (f32[32,256]{1,0:T(8,128)S(1)}, f32[32,256]{1,0:T(8,128)}, u32[]{:S(2)}) copy-start(f32[32,256]{1,0:T(8,128)} %constant.58.clone) | copy-start | bytes 98308
  138.2 4.6 %copy-start.8 = (f32[32,256]{1,0:T(8,128)S(1)}, f32[32,256]{1,0:T(8,128)}, u32[]{:S(2)}) copy-start(f32[32,256]{1,0:T(8,128)} %constant.59.clone) | copy-start | bytes 98308
Sparse Core Ops, SparseCore 0:
  75.0 63.1 all-gather.2
